TPU v7x, 32 devices: a whole 2x2x4 slice. The times are simulated.
32 devices in a mesh: space: 4 (over y, x), scen: 8 (over z, core).
Axes of the slice: x: 2, y: 2, z: 4, core: 2. Of those that a mesh axis runs over, the one named last changes fastest.
Arguments:
- tracers: float32 [8, 2, 20, 32, 512], P('scen', None, None, None, 'space'), may hold values from -6 to 6
- diffusivity: float32 [2, 20, 32, 512], P(None, None, 'scen', 'space'), may hold values from 0.02 to 0.16
- level_count: int32 [32, 512], P(None, 'space'), may hold values from 0 to 20
- shelf_mask: int32 [32, 512], P(None, 'space'), may hold values 0 or 1
- cotangent: float32 [8, 2, 20, 32, 512], P('scen', None, None, None, 'space'), may hold values from -6 to 6
Outputs:
- final_tracers: float32 [8, 2, 20, 32, 512], P('scen', None, None, None, 'space')
- adjoint_tracers: float32 [8, 2, 20, 32, 512], P('scen', None, None, None, 'space')
- kappa_grad: float32 [2, 20, 32, 512], P(None, None, 'scen', 'space')
Inputs may be any that keep to these rules, and one draw needn't show every extreme that they name: `level_count`: wet levels of a column, counted from the surface; 0 marks land.
All inputs are finite; a program needn't handle non-finite values. No bound on the sum of `shelf_mask` on one device may be relied on, other than what follows from the above.
Results may differ from a plain program's by a relative error of at most 0.00002.
Values sent between devices are 32-bit elements; how exact they have to be, the bound alone decides.
No kernel may reach another device: no remote copies, remote signals or barrier semaphores. Data moves between devices by JAX's collectives and lax.ppermute only.
A program may use at most 64 MiB of HBM per device.

v0:
```python
import jax
import jax.numpy as jnp
from jax import lax
from jax.sharding import PartitionSpec as P

STEPS = 2
vertical_rate = 0.1
thaw_rate = 0.3


def with_halo(block, sides, width):
    for axis, dim in sides:
        count = lax.axis_size(axis)
        forward = [(i, i + 1) for i in range(count - 1)]
        forward.append((count - 1, 0))
        backward = [(target, source) for source, target in forward]
        low = lax.ppermute(
            lax.slice_in_dim(block, block.shape[dim] - width, None, axis=dim), axis, forward
        )
        high = lax.ppermute(lax.slice_in_dim(block, 0, width, axis=dim), axis, backward)
        block = jnp.concatenate([low, block, high], axis=dim)
    return block


def from_partner(value, axis, stride):
    return lax.ppermute(value, axis, [(i, i ^ 1 << stride) for i in range(lax.axis_size(axis))])


def with_edges(field_now):
    return with_halo(field_now, (("space", 3),), 1)


def partner_row(top_row):
    exchanged = top_row
    for bit_index in range(lax.axis_size("space").bit_length() - 1):
        exchanged = from_partner(exchanged, "space", bit_index)
    return exchanged[:, :, ::-1]


def sources_of(wetness, shelf_mask):
    below_wet = jnp.concatenate([wetness[1:], jnp.zeros_like(wetness[:1])], axis=0)
    heat_source = thaw_rate * shelf_mask.astype(jnp.float32)[None] * wetness * (1.0 - below_wet)
    return jnp.stack([heat_source, jnp.zeros_like(heat_source)])


def operate_on(tracer_now, coeffs):
    east_coeff, north_coeff, fold_coeff, down_coeff = coeffs
    edged_field = with_edges(tracer_now)
    east_flux = east_coeff * (edged_field[..., 1:] - edged_field[..., :-1])
    across_x = east_flux[..., 1:] - east_flux[..., :-1]
    north_flux = north_coeff * (tracer_now[:, :, 1:] - tracer_now[:, :, :-1])
    top_row = tracer_now[:, :, -1]
    partner = partner_row(top_row)
    fold_flux = fold_coeff * (partner - top_row)
    all_north = jnp.concatenate([north_flux, fold_flux[:, :, None]], axis=2)
    zero_row = jnp.zeros_like(all_north[:, :, :1])
    across_y = all_north - jnp.concatenate([zero_row, all_north[:, :, :-1]], axis=2)
    down_flux = down_coeff * (tracer_now[:, 1:] - tracer_now[:, :-1])
    zero_level = jnp.zeros_like(down_flux[:, :1])
    across_z = jnp.concatenate([down_flux, zero_level], axis=1) - jnp.concatenate(
        [zero_level, down_flux], axis=1
    )
    return (across_x + across_y + across_z, edged_field, partner)


def on_device(tracers, diffusivity, level_count, shelf_mask, cotangent):
    full_kappa = lax.all_gather(diffusivity, "scen", axis=2, tiled=True)
    levels = lax.broadcasted_iota(jnp.int32, (full_kappa.shape[1],) + level_count.shape, 0)
    wetness = (levels < level_count[None]).astype(jnp.float32)
    sources = sources_of(wetness, shelf_mask)
    edged_coeff = with_edges(jnp.stack([wetness, full_kappa[0]]))
    wet_edge = edged_coeff[0]
    kappa_edge = edged_coeff[1]
    east_mask = wet_edge[..., :-1] * wet_edge[..., 1:]
    east_coeff = kappa_edge[..., :-1] * east_mask
    north_kappa = full_kappa[1]
    north_mask = wetness[:, :-1] * wetness[:, 1:]
    north_coeff = north_kappa[:, :-1] * north_mask
    top_wet = wetness[:, -1]
    top_kappa = north_kappa[:, -1]
    partner_coeff = partner_row(jnp.stack([top_wet, top_kappa]))
    fold_mask = top_wet * partner_coeff[0]
    fold_coeff = 0.5 * (top_kappa + partner_coeff[1]) * fold_mask
    down_coeff = vertical_rate * wetness[:-1] * wetness[1:]
    coeffs = (east_coeff, north_coeff, fold_coeff, down_coeff)
    tracer_now = tracers[0]
    stored = []
    for substep in range(STEPS):
        change, edged_field, partner = operate_on(tracer_now, coeffs)
        stored.append((tracer_now, edged_field, partner))
        tracer_now = wetness * (tracer_now + change + sources)
    adjoint = cotangent[0]
    summed = None
    for substep in reversed(range(STEPS)):
        weighted = wetness * adjoint
        change, weighted_edge, weighted_partner = operate_on(weighted, coeffs)
        adjoint = weighted + change
        before, before_edge, before_partner = stored[substep]
        grad_east = jnp.sum(
            east_mask[..., 1:]
            * (before_edge[..., 2:] - before_edge[..., 1:-1])
            * (weighted_edge[..., 1:-1] - weighted_edge[..., 2:]),
            axis=0,
        )
        grad_inner = jnp.sum(
            north_mask
            * (before[:, :, 1:] - before[:, :, :-1])
            * (weighted[:, :, :-1] - weighted[:, :, 1:]),
            axis=0,
        )
        grad_fold = jnp.sum(
            0.5
            * fold_mask
            * (before_partner - before[:, :, -1])
            * (weighted[:, :, -1] - weighted_partner),
            axis=0,
        )
        grad_term = jnp.stack(
            [grad_east, jnp.concatenate([grad_inner, grad_fold[:, None]], axis=1)]
        )
        summed = grad_term if summed is None else summed + grad_term
    kappa_grad = lax.psum_scatter(summed, "scen", scatter_dimension=2, tiled=True)
    return (tracer_now[None], adjoint[None], kappa_grad)


def solution(mesh):
    placed = (
        P("scen", None, None, None, "space"),
        P(None, None, "scen", "space"),
        P(None, "space"),
        P(None, "space"),
        P("scen", None, None, None, "space"),
    )
    return jax.shard_map(
        on_device,
        mesh=mesh,
        in_specs=placed,
        out_specs=(
            P("scen", None, None, None, "space"),
            P("scen", None, None, None, "space"),
            P(None, None, "scen", "space"),
        ),
        check_vma=False,
    )
```

profile of v0, /device:TPU:0, one launch (start us, length us, event | category | flops | bytes accessed | tf_op | source)
XLA Modules:
  0.0 178.3 jit_solution(11726017105144906224)
XLA Ops:
  8.9 17.0 %all_gather.3 = f32[2,20,32,128]{3,0,1,2:T(2,128)S(1)} all-gather(f32[2,20,4,128]{3,0,1,2:T(2,128)S(1)} %copy.135), channel_id=1, replica_groups=mesh['space'=4,'scen'=8] {'scen'}, dimensions={2}, use_global_device_ids=true | all-gather | bytes 737280 | tf_op jit(solution)/shard_map/all_gather | solution.py:67
  25.9 1.2 fusion.47
  27.2 1.6 collective-permute-start.4
  30.9 1.5 collective-permute-start.2
  35.5 2.4 %collective-permute-start.1 = (f32[2,20,32,1]{2,0,3,1:T(2,128)}, f32[2,20,32,1]{2,0,3,1:T(2,128)}, u32[]{:S(2)}, u32[]{:S(2)}) collective-permute-start(f32[2,20,32,1]{2,0,3,1:T(2,128)} %copy.138), channel_id=1, source_target_pairs={{8,0},{16,8},{24,16},{0,24},{9,1},{17,9},{25,17},{1,25},{10,2},{18... | collective-permute-start | bytes 15368 | tf_op jit(solution)/shard_map/ppermute | solution.py:20
  40.9 1.7 fusion.45
  43.1 1.6 fusion.38
  44.8 1.6 subtract_multiply_fusion.1
  46.5 1.1 copy.149
  48.5 2.0 %copy.157 = f32[2,20,32,1]{2,0,3,1:T(2,128)} copy(f32[2,20,32,1]{3,0,1,2:T(2,128)} %get-tuple-element.37) | data formatting | bytes 10240 | tf_op jit(solution)/shard_map/slice | solution.py:18
  51.4 2.9 %collective-permute-start.12 = (f32[2,20,32,1]{2,0,3,1:T(2,128)}, f32[2,20,32,1]{2,0,3,1:T(2,128)}, u32[]{:S(2)}, u32[]{:S(2)}) collective-permute-start(f32[2,20,32,1]{2,0,3,1:T(2,128)} %copy.155), channel_id=1, source_target_pairs={{8,0},{16,8},{24,16},{0,24},{9,1},{17,9},{25,17},{1,25},{10,2},{18... | collective-permute-start | bytes 15368 | tf_op jit(solution)/shard_map/ppermute | solution.py:20
  54.3 1.0 copy.139
  55.6 1.9 %copy.140 = f32[2,20,32,1]{3,2,1,0:T(8,128)} copy(f32[2,20,32,1]{2,0,3,1:T(2,128)} %collective-permute-done.1) | data formatting | bytes 10240 | tf_op jit(solution)/shard_map/ppermute | solution.py:20
  57.5 1.7 pad_maximum_fusion.4
  59.2 1.1 slice_multiply_fusion.1
  60.7 2.0 %collective-permute-start.14 = (f32[2,20,128]{2,0,1:T(2,128)S(1)}, f32[2,20,128]{2,0,1:T(2,128)}, u32[]{:S(2)}, u32[]{:S(2)}) collective-permute-start(f32[2,20,128]{2,0,1:T(2,128)S(1)} %slice_bitcast_fusion.3), channel_id=1, source_target_pairs={{0,8},{8,0},{16,24},{24,16},{1,9},{9,1},{17,25},{25,17},{2,10},{10... | collective-permute-start | bytes 61448 | tf_op jit(solution)/shard_map/ppermute | solution.py:26
  63.4 1.2 copy.145
  64.5 1.9 %copy.156 = f32[2,20,32,1]{3,0,1,2:T(2,128)} copy(f32[2,20,32,1]{2,0,3,1:T(2,128)} %collective-permute-done.12) | data formatting | bytes 10240 | tf_op jit(solution)/shard_map/ppermute | solution.py:20
  66.4 1.9 %copy.158 = f32[2,20,32,1]{3,0,1,2:T(2,128)} copy(f32[2,20,32,1]{2,0,3,1:T(2,128)} %collective-permute-done.13) | data formatting | bytes 10240 | tf_op jit(solution)/shard_map/ppermute | solution.py:17
  68.3 1.5 collective-permute-start.5
  69.8 5.6 %fusion.3 = (f32[2,20,32,129]{3,0,1,2:T(2,128)}, f32[2,20,32,129]{3,0,1,2:T(2,128)}) fusion(f32[2,20,32,1]{3,0,1,2:T(2,128)} %copy.156, f32[2,20,32,128]{3,0,1,2:T(2,128)S(1)} %bitcast_multiply_fusion, f32[2,20,32,1]{3,0,1,2:T(2,128)} %copy.158, f32[20,32,129]{2,0,1:T(8,128)S(1)} %copy.141, f32[2,20,32,128]{3,0,1,2:T(2,128)S(1)} %bitcast.82, ...), kind=kLoop, calls=%fused_computation.15 | loop fusion | flops 1320960 | bytes 2982400 | tf_op jit(solution)/shard_map/mul | solution.py:49
  77.0 1.5 collective-permute-start.7
  78.8 1.6 collective-permute-done.15
  81.0 6.4 %fusion.33 = (f32[2,20,32,128]{3,0,1,2:T(2,128)S(1)}, f32[2,20,32,128]{3,0,1,2:T(2,128)S(1)}) fusion(f32[2,19,32,128]{3,0,1,2:T(2,128)} %get-tuple-element.51, f32[2,20,31,128]{3,0,1,2:T(2,128)} %get-tuple-element.53, f32[2,20,1,128]{3,0,1,2:T(2,128)S(1)} %get-tuple-element.61, f32[2,20,32,129]{3,0,1,2:T(2,128)} %get-tuple-element.29, ...), kind=kLoop, calls=%fused_computation.65 | loop fusion | flops 2949120 | bytes 8454144 | tf_op jit(solution)/shard_map/mul | solution.py:95
  87.4 1.7 fusion.44
  89.1 1.8 fusion.46
  90.9 2.0 %collective-permute-start.10 = (f32[2,20,128]{2,0,1:T(2,128)S(1)}, f32[2,20,128]{2,0,1:T(2,128)}, u32[]{:S(2)}, u32[]{:S(2)}) collective-permute-start(f32[2,20,128]{2,0,1:T(2,128)S(1)} %slice_bitcast_fusion.4), channel_id=1, source_target_pairs={{0,8},{8,0},{16,24},{24,16},{1,9},{9,1},{17,25},{25,17},{2,10},{10... | collective-permute-start | bytes 61448 | tf_op jit(solution)/shard_map/ppermute | solution.py:26
  92.9 6.6 %multiply_reduce_fusion = (f32[20,31,128]{2,0,1:T(8,128)}, f32[20,31,128]{2,0,1:T(8,128)}, f32[2,20,31,128]{3,0,1,2:T(2,128)}, f32[2,20,31,128]{3,0,1,2:T(2,128)}) fusion(f32[2,20,32,128]{3,0,1,2:T(2,128)S(1)} %get-tuple-element.49, f32[20,31,128]{2,0,1:T(8,128)S(1)} %copy-done.18, f32[2,20,32,128]{3,0,1,2:T(2,128)S(1)} %bitcast.84, ...), kind=kLoop, calls=%fused_computation.71 | loop fusion | flops 1904640 | bytes 7618560 | tf_op jit(solution)/shard_map/reduce_sum | solution.py:105
  99.5 2.0 %copy.159 = f32[2,20,32,1]{2,0,3,1:T(2,128)} copy(f32[2,20,32,1]{3,0,1,2:T(2,128)} %get-tuple-element.36) | data formatting | bytes 10240 | tf_op jit(solution)/shard_map/slice | solution.py:20
  101.5 2.9 %collective-permute-start.16 = (f32[2,20,32,1]{2,0,3,1:T(2,128)}, f32[2,20,32,1]{2,0,3,1:T(2,128)}, u32[]{:S(2)}, u32[]{:S(2)}) collective-permute-start(f32[2,20,32,1]{2,0,3,1:T(2,128)} %copy.159), channel_id=1, source_target_pairs={{8,0},{16,8},{24,16},{0,24},{9,1},{17,9},{25,17},{1,25},{10,2},{18... | collective-permute-start | bytes 15368 | tf_op jit(solution)/shard_map/ppermute | solution.py:20
  104.4 2.0 %copy.150 = f32[2,20,32,1]{2,0,3,1:T(2,128)} copy(f32[2,20,32,1]{3,0,1,2:T(2,128)} %get-tuple-element.40) | data formatting | bytes 10240 | tf_op jit(solution)/shard_map/slice | solution.py:20
  106.4 2.7 %fusion.37 = (f32[2,19,32,128]{3,0,1,2:T(2,128)}, f32[2,19,32,128]{3,0,1,2:T(2,128)}) fusion(f32[2,20,32,128]{3,0,1,2:T(2,128)S(1)} %get-tuple-element.49, f32[19,32,128]{2,0,1:T(8,128)} %copy-done.5, f32[2,20,32,128]{3,0,1,2:T(2,128)S(1)} %get-tuple-element.50), kind=kLoop, calls=%fused_computation.76 | loop fusion | flops 622592 | bytes 4046848 | tf_op jit(solution)/shard_map/mul | solution.py:58
  109.2 1.4 copy.161
  110.6 2.0 %collective-permute-start.17 = (f32[2,20,32,1]{2,0,3,1:T(2,128)S(1)}, f32[2,20,32,1]{2,0,3,1:T(2,128)}, u32[]{:S(2)}, u32[]{:S(2)}) collective-permute-start(f32[2,20,32,1]{2,0,3,1:T(2,128)S(1)} %copy.161), channel_id=1, source_target_pairs={{0,8},{8,16},{16,24},{24,0},{1,9},{9,17},{17,25},{25,1},{2,10},{10... | collective-permute-start | bytes 15368 | tf_op jit(solution)/shard_map/ppermute | solution.py:17
  112.6 2.0 %copy.152 = f32[2,20,32,1]{2,0,3,1:T(2,128)} copy(f32[2,20,32,1]{3,0,1,2:T(2,128)} %get-tuple-element.39) | data formatting | bytes 10240 | tf_op jit(solution)/shard_map/slice | solution.py:18
  114.6 1.9 %copy.160 = f32[2,20,32,1]{3,0,1,2:T(2,128)} copy(f32[2,20,32,1]{2,0,3,1:T(2,128)} %collective-permute-done.16) | data formatting | bytes 10240 | tf_op jit(solution)/shard_map/ppermute | solution.py:20
  116.5 1.9 %copy.151 = f32[2,20,32,1]{3,0,1,2:T(2,128)} copy(f32[2,20,32,1]{2,0,3,1:T(2,128)} %collective-permute-done.8) | data formatting | bytes 10240 | tf_op jit(solution)/shard_map/ppermute | solution.py:20
  118.4 1.5 collective-permute-start.11
  120.4 8.7 %fusion.36 = (f32[20,32,128]{2,0,1:T(8,128)}, f32[20,32,128]{2,0,1:T(8,128)}) fusion(f32[2,20,32,128]{3,0,1,2:T(2,128)S(1)} %get-tuple-element.49, f32[2,20,32,1]{3,0,1,2:T(2,128)} %copy.160, f32[2,20,32,128]{3,0,1,2:T(2,128)S(1)} %bitcast.85, f32[2,20,32,1]{3,0,1,2:T(2,128)} %copy-done.2, f32[20,32,128]{2,0,1:T(8,128)} %copy.163, ...), kind=kLoop, calls=%fused_computation.68 | loop fusion | flops 2129920 | bytes 3624960 | tf_op jit(solution)/shard_map/reduce_sum | solution.py:99
  129.1 1.9 %copy.162 = f32[2,20,32,1]{3,0,1,2:T(2,128)} copy(f32[2,20,32,1]{2,0,3,1:T(2,128)} %collective-permute-done.17) | data formatting | bytes 10240 | tf_op jit(solution)/shard_map/ppermute | solution.py:17
  131.0 1.9 %copy.153 = f32[2,20,32,1]{3,0,1,2:T(2,128)} copy(f32[2,20,32,1]{2,0,3,1:T(2,128)} %collective-permute-done.9) | data formatting | bytes 10240 | tf_op jit(solution)/shard_map/ppermute | solution.py:17
  133.3 1.1 maximum_bitcast_fusion.1
  134.3 1.0 maximum_bitcast_fusion
  137.1 4.8 %fusion.1 = (f32[2,20,32,129]{3,0,1,2:T(2,128)S(1)}, f32[2,20,32,129]{3,0,1,2:T(2,128)S(1)}) fusion(f32[2,20,32,1]{3,0,1,2:T(2,128)S(1)} %copy-done.3, f32[2,20,32,128]{3,0,1,2:T(2,128)S(1)} %get-tuple-element.49, f32[2,20,32,1]{3,0,1,2:T(2,128)} %copy.162, f32[20,32,129]{2,0,1:T(8,128)S(1)} %copy.141, f32[2,20,32,128]{3,0,1,2:T(2,128)S(1)} %get-tuple-element.50, ...), kind=kLoop, calls=%fused_computation.13 | loop fusion | flops 1320960 | bytes 2982400 | tf_op jit(solution)/shard_map/mul | solution.py:49
  141.9 1.4 fusion.34
  144.7 1.6 fusion.10
  147.3 22.6 %reduce-scatter.2.cloned.1.call-done = f32[2,20,4,128]{3,1,0,2:T(8,128)} async-done(((f32[2,20,32,128]{3,1,0,2:T(8,128)}), f32[2,20,4,128]{3,1,0,2:T(8,128)}) %reduce-scatter.2.cloned.1.call-update) | async-done | bytes 81936 | tf_op jit(solution)/shard_map/reduce_scatter | solution.py:122
  169.9 1.6 copy.168
  (123 shorter events, 21.1 us)
Async XLA Ops:
  7.2 162.7 %reduce-scatter.2.cloned.1.call-start = ((), (), s32[]{:S(2)}) async-start(), calls=%async_computation.1 | async-start | bytes 884736 | tf_op jit(solution)/shard_map/reduce_scatter | solution.py:122
  8.9 19.9 %copy-start.10 = (f32[1,2,20,32,128]{4,3,2,1,0:T(8,128)S(1)}, f32[1,2,20,32,128]{4,3,2,1,0:T(8,128)}, u32[]{:S(2)}) copy-start(f32[1,2,20,32,128]{4,3,2,1,0:T(8,128)} %param.5) | copy-start | bytes 1966084
  27.2 41.1 %collective-permute-start.4 = (f32[2,20,128]{2,0,1:T(2,128)S(1)}, f32[2,20,128]{2,0,1:T(2,128)}, u32[]{:S(2)}, u32[]{:S(2)}) collective-permute-start(f32[2,20,128]{2,0,1:T(2,128)S(1)} %pad_maximum_fusion.6), channel_id=1, source_target_pairs={{0,8},{8,0},{16,24},{24,16},{1,9},{9,1},{17,25},{25,17},{2,10},{10... | collective-permute-start | bytes 61448 | tf_op jit(solution)/shard_map/ppermute | solution.py:26
  30.0 3.3 %copy-start.20 = (s32[32,128]{1,0:T(8,128)S(1)}, s32[32,128]{1,0:T(8,128)}, u32[]{:S(2)}) copy-start(s32[32,128]{1,0:T(8,128)} %param.7) | copy-start | bytes 49156
  30.9 29.8 %collective-permute-start.2 = (f32[2,20,32,1]{2,0,3,1:T(2,128)}, f32[2,20,32,1]{2,0,3,1:T(2,128)S(1)}, u32[]{:S(2)}, u32[]{:S(2)}) collective-permute-start(f32[2,20,32,1]{2,0,3,1:T(2,128)} %copy.142), channel_id=1, source_target_pairs={{8,0},{16,8},{24,16},{0,24},{9,1},{17,9},{25,17},{1,25},{10,2},{18... | collective-permute-start | bytes 15368 | tf_op jit(solution)/shard_map/ppermute | solution.py:20
  32.7 30.5 %collective-permute-start.3 = (f32[2,20,32,1]{2,0,3,1:T(2,128)S(1)}, f32[2,20,32,1]{2,0,3,1:T(2,128)S(1)}, u32[]{:S(2)}, u32[]{:S(2)}) collective-permute-start(f32[2,20,32,1]{2,0,3,1:T(2,128)S(1)} %copy.144), channel_id=1, source_target_pairs={{0,8},{8,16},{16,24},{24,0},{1,9},{9,17},{17,25},{25,1},{2,10},{10... | collective-permute-start | bytes 15368 | tf_op jit(solution)/shard_map/ppermute | solution.py:17
  35.5 19.8 %collective-permute-start.1 = (f32[2,20,32,1]{2,0,3,1:T(2,128)}, f32[2,20,32,1]{2,0,3,1:T(2,128)}, u32[]{:S(2)}, u32[]{:S(2)}) collective-permute-start(f32[2,20,32,1]{2,0,3,1:T(2,128)} %copy.138), channel_id=1, source_target_pairs={{8,0},{16,8},{24,16},{0,24},{9,1},{17,9},{25,17},{1,25},{10,2},{18... | collective-permute-start | bytes 15368 | tf_op jit(solution)/shard_map/ppermute | solution.py:20
  38.8 12.6 %collective-permute-start = (f32[2,20,32,1]{2,0,3,1:T(2,128)}, f32[2,20,32,1]{2,0,3,1:T(2,128)}, u32[]{:S(2)}, u32[]{:S(2)}) collective-permute-start(f32[2,20,32,1]{2,0,3,1:T(2,128)} %copy.137), channel_id=1, source_target_pairs={{0,8},{8,16},{16,24},{24,0},{1,9},{9,17},{17,25},{25,1},{2,10},{10... | collective-permute-start | bytes 15368 | tf_op jit(solution)/shard_map/ppermute | solution.py:17
  39.0 0.7 copy-start
  39.0 1.2 copy-start.9
  40.9 1.8 copy-start.21
  42.9 1.9 %copy-start.6 = (f32[20,31,128]{2,0,1:T(8,128)}, f32[20,31,128]{2,0,1:T(8,128)S(1)}, u32[]{:S(2)}) copy-start(f32[20,31,128]{2,0,1:T(8,128)S(1)} %copy.147) | copy-start | bytes 952324
  43.1 1.7 copy-start.5
  46.4 4.1 %copy-start.11 = (f32[2,20,32,1]{3,0,1,2:T(2,128)S(1)}, f32[2,20,32,1]{3,0,1,2:T(2,128)}, u32[]{:S(2)}) copy-start(f32[2,20,32,1]{3,0,1,2:T(2,128)} %get-tuple-element.38) | copy-start | bytes 15364
  51.4 13.2 %collective-permute-start.12 = (f32[2,20,32,1]{2,0,3,1:T(2,128)}, f32[2,20,32,1]{2,0,3,1:T(2,128)}, u32[]{:S(2)}, u32[]{:S(2)}) collective-permute-start(f32[2,20,32,1]{2,0,3,1:T(2,128)} %copy.155), channel_id=1, source_target_pairs={{8,0},{16,8},{24,16},{0,24},{9,1},{17,9},{25,17},{1,25},{10,2},{18... | collective-permute-start | bytes 15368 | tf_op jit(solution)/shard_map/ppermute | solution.py:20
  55.4 11.1 %collective-permute-start.13 = (f32[2,20,32,1]{2,0,3,1:T(2,128)}, f32[2,20,32,1]{2,0,3,1:T(2,128)}, u32[]{:S(2)}, u32[]{:S(2)}) collective-permute-start(f32[2,20,32,1]{2,0,3,1:T(2,128)} %copy.157), channel_id=1, source_target_pairs={{0,8},{8,16},{16,24},{24,0},{1,9},{9,17},{17,25},{25,1},{2,10},{10... | collective-permute-start | bytes 15368 | tf_op jit(solution)/shard_map/ppermute | solution.py:17
  60.7 15.7 %collective-permute-start.14 = (f32[2,20,128]{2,0,1:T(2,128)S(1)}, f32[2,20,128]{2,0,1:T(2,128)}, u32[]{:S(2)}, u32[]{:S(2)}) collective-permute-start(f32[2,20,128]{2,0,1:T(2,128)S(1)} %slice_bitcast_fusion.3), channel_id=1, source_target_pairs={{0,8},{8,0},{16,24},{24,16},{1,9},{9,1},{17,25},{25,17},{2,10},{10... | collective-permute-start | bytes 61448 | tf_op jit(solution)/shard_map/ppermute | solution.py:26
  63.2 12.1 %copy-start.2 = (f32[2,20,32,1]{3,0,1,2:T(2,128)}, f32[2,20,32,1]{3,0,1,2:T(2,128)S(1)}, u32[]{:S(2)}) copy-start(f32[2,20,32,1]{3,0,1,2:T(2,128)S(1)} %copy.143) | copy-start | bytes 15364
  63.2 13.8 %collective-permute-start.6 = (f32[2,20,128]{2,0,1:T(2,128)S(1)}, f32[2,20,128]{2,0,1:T(2,128)S(1)}, u32[]{:S(2)}, u32[]{:S(2)}) collective-permute-start(f32[2,20,128]{2,0,1:T(2,128)S(1)} %slice_bitcast_fusion.5), channel_id=1, source_target_pairs={{0,8},{8,0},{16,24},{24,16},{1,9},{9,1},{17,25},{25,17},{2,10},{10... | collective-permute-start | bytes 61448 | tf_op jit(solution)/shard_map/ppermute | solution.py:26
  68.3 7.0 %copy-start.19 = (f32[20,32,129]{2,1,0:T(8,128)S(1)}, f32[20,32,129]{2,1,0:T(8,128)}, u32[]{:S(2)}) copy-start(f32[20,32,129]{2,1,0:T(8,128)} %get-tuple-element.24) | copy-start | bytes 990724
  68.3 10.2 %collective-permute-start.5 = (f32[2,20,128]{2,0,1:T(2,128)}, f32[2,20,128]{2,0,1:T(2,128)S(1)}, u32[]{:S(2)}, u32[]{:S(2)}) collective-permute-start(f32[2,20,128]{2,0,1:T(2,128)} %collective-permute-done.4), channel_id=1, source_target_pairs={{0,16},{8,24},{16,0},{24,8},{1,17},{9,25},{17,1},{25,9},{2,18},{10... | collective-permute-start | bytes 61448 | tf_op jit(solution)/shard_map/ppermute | solution.py:26
  76.5 4.0 %collective-permute-start.15 = (f32[2,20,128]{2,0,1:T(2,128)}, f32[2,20,128]{2,0,1:T(2,128)S(1)}, u32[]{:S(2)}, u32[]{:S(2)}) collective-permute-start(f32[2,20,128]{2,0,1:T(2,128)} %collective-permute-done.14), channel_id=1, source_target_pairs={{0,16},{8,24},{16,0},{24,8},{1,17},{9,25},{17,1},{25,9},{2,18},{10... | collective-permute-start | bytes 61448 | tf_op jit(solution)/shard_map/ppermute | solution.py:26
  77.0 3.8 %collective-permute-start.7 = (f32[2,20,128]{2,0,1:T(2,128)S(1)}, f32[2,20,128]{2,0,1:T(2,128)S(1)}, u32[]{:S(2)}, u32[]{:S(2)}) collective-permute-start(f32[2,20,128]{2,0,1:T(2,128)S(1)} %collective-permute-done.6), channel_id=1, source_target_pairs={{0,16},{8,24},{16,0},{24,8},{1,17},{9,25},{17,1},{25,9},{2,18},{10... | collective-permute-start | bytes 61448 | tf_op jit(solution)/shard_map/ppermute | solution.py:26
  89.1 3.8 %copy-start.7 = (f32[20,31,128]{2,0,1:T(8,128)S(1)}, f32[20,31,128]{2,0,1:T(8,128)}, u32[]{:S(2)}) copy-start(f32[20,31,128]{2,0,1:T(8,128)} %copy-done.6) | copy-start | bytes 952324
  89.1 3.8 %copy-start.18 = (f32[20,31,128]{2,0,1:T(8,128)S(1)}, f32[20,31,128]{2,0,1:T(8,128)}, u32[]{:S(2)}) copy-start(f32[20,31,128]{2,0,1:T(8,128)} %copy.164) | copy-start | bytes 952324
  90.9 27.5 %collective-permute-start.10 = (f32[2,20,128]{2,0,1:T(2,128)S(1)}, f32[2,20,128]{2,0,1:T(2,128)}, u32[]{:S(2)}, u32[]{:S(2)}) collective-permute-start(f32[2,20,128]{2,0,1:T(2,128)S(1)} %slice_bitcast_fusion.4), channel_id=1, source_target_pairs={{0,8},{8,0},{16,24},{24,16},{1,9},{9,1},{17,25},{25,17},{2,10},{10... | collective-permute-start | bytes 61448 | tf_op jit(solution)/shard_map/ppermute | solution.py:26
  92.9 27.0 %collective-permute-start.18 = (f32[2,20,128]{2,0,1:T(2,128)S(1)}, f32[2,20,128]{2,0,1:T(2,128)}, u32[]{:S(2)}, u32[]{:S(2)}) collective-permute-start(f32[2,20,128]{2,0,1:T(2,128)S(1)} %slice_bitcast_fusion.2), channel_id=1, source_target_pairs={{0,8},{8,0},{16,24},{24,16},{1,9},{9,1},{17,25},{25,17},{2,10},{10... | collective-permute-start | bytes 61448 | tf_op jit(solution)/shard_map/ppermute | solution.py:26
  101.5 13.1 %collective-permute-start.16 = (f32[2,20,32,1]{2,0,3,1:T(2,128)}, f32[2,20,32,1]{2,0,3,1:T(2,128)}, u32[]{:S(2)}, u32[]{:S(2)}) collective-permute-start(f32[2,20,32,1]{2,0,3,1:T(2,128)} %copy.159), channel_id=1, source_target_pairs={{8,0},{16,8},{24,16},{0,24},{9,1},{17,9},{25,17},{1,25},{10,2},{18... | collective-permute-start | bytes 15368 | tf_op jit(solution)/shard_map/ppermute | solution.py:20
  106.4 10.1 %collective-permute-start.8 = (f32[2,20,32,1]{2,0,3,1:T(2,128)}, f32[2,20,32,1]{2,0,3,1:T(2,128)}, u32[]{:S(2)}, u32[]{:S(2)}) collective-permute-start(f32[2,20,32,1]{2,0,3,1:T(2,128)} %copy.150), channel_id=1, source_target_pairs={{8,0},{16,8},{24,16},{0,24},{9,1},{17,9},{25,17},{1,25},{10,2},{18... | collective-permute-start | bytes 15368 | tf_op jit(solution)/shard_map/ppermute | solution.py:20
  110.6 18.5 %collective-permute-start.17 = (f32[2,20,32,1]{2,0,3,1:T(2,128)S(1)}, f32[2,20,32,1]{2,0,3,1:T(2,128)}, u32[]{:S(2)}, u32[]{:S(2)}) collective-permute-start(f32[2,20,32,1]{2,0,3,1:T(2,128)S(1)} %copy.161), channel_id=1, source_target_pairs={{0,8},{8,16},{16,24},{24,0},{1,9},{9,17},{17,25},{25,1},{2,10},{10... | collective-permute-start | bytes 15368 | tf_op jit(solution)/shard_map/ppermute | solution.py:17
  114.6 16.4 %collective-permute-start.9 = (f32[2,20,32,1]{2,0,3,1:T(2,128)}, f32[2,20,32,1]{2,0,3,1:T(2,128)}, u32[]{:S(2)}, u32[]{:S(2)}) collective-permute-start(f32[2,20,32,1]{2,0,3,1:T(2,128)} %copy.152), channel_id=1, source_target_pairs={{0,8},{8,16},{16,24},{24,0},{1,9},{9,17},{17,25},{25,1},{2,10},{10... | collective-permute-start | bytes 15368 | tf_op jit(solution)/shard_map/ppermute | solution.py:17
  118.4 14.5 %collective-permute-start.11 = (f32[2,20,128]{2,0,1:T(2,128)}, f32[2,20,128]{2,0,1:T(2,128)S(1)}, u32[]{:S(2)}, u32[]{:S(2)}) collective-permute-start(f32[2,20,128]{2,0,1:T(2,128)} %collective-permute-done.10), channel_id=1, source_target_pairs={{0,16},{8,24},{16,0},{24,8},{1,17},{9,25},{17,1},{25,9},{2,18},{10... | collective-permute-start | bytes 61448 | tf_op jit(solution)/shard_map/ppermute | solution.py:26
  119.8 13.1 %collective-permute-start.19 = (f32[2,20,128]{2,0,1:T(2,128)}, f32[2,20,128]{2,0,1:T(2,128)S(1)}, u32[]{:S(2)}, u32[]{:S(2)}) collective-permute-start(f32[2,20,128]{2,0,1:T(2,128)} %collective-permute-done.18), channel_id=1, source_target_pairs={{0,16},{8,24},{16,0},{24,8},{1,17},{9,25},{17,1},{25,9},{2,18},{10... | collective-permute-start | bytes 61448 | tf_op jit(solution)/shard_map/ppermute | solution.py:26
  133.1 2.2 %copy-start.16 = (f32[20,32,128]{2,0,1:T(8,128)S(1)}, f32[20,32,128]{2,0,1:T(8,128)}, u32[]{:S(2)}) copy-start(f32[20,32,128]{2,0,1:T(8,128)} %get-tuple-element.15) | copy-start | bytes 983044
  133.1 2.2 %copy-start.17 = (f32[20,32,128]{2,0,1:T(8,128)S(1)}, f32[20,32,128]{2,0,1:T(8,128)}, u32[]{:S(2)}) copy-start(f32[20,32,128]{2,0,1:T(8,128)} %get-tuple-element.16) | copy-start | bytes 983044
  135.5 1.4 copy-start.3
  135.5 1.6 copy-start.4
  137.1 4.8 %copy-start.13 = (f32[2,20,31,128]{3,0,1,2:T(2,128)S(1)}, f32[2,20,31,128]{3,0,1,2:T(2,128)}, u32[]{:S(2)}) copy-start(f32[2,20,31,128]{3,0,1,2:T(2,128)} %get-tuple-element.34) | copy-start | bytes 1904644
  137.1 4.8 %copy-start.15 = (f32[2,19,32,128]{3,0,1,2:T(2,128)S(1)}, f32[2,19,32,128]{3,0,1,2:T(2,128)}, u32[]{:S(2)}) copy-start(f32[2,19,32,128]{3,0,1,2:T(2,128)} %get-tuple-element.47) | copy-start | bytes 1867780
  141.9 2.4 %copy-start.12 = (f32[2,20,31,128]{3,0,1,2:T(2,128)S(1)}, f32[2,20,31,128]{3,0,1,2:T(2,128)}, u32[]{:S(2)}) copy-start(f32[2,20,31,128]{3,0,1,2:T(2,128)} %get-tuple-element.33) | copy-start | bytes 1904644
  141.9 2.4 %copy-start.14 = (f32[2,19,32,128]{3,0,1,2:T(2,128)S(1)}, f32[2,19,32,128]{3,0,1,2:T(2,128)}, u32[]{:S(2)}) copy-start(f32[2,19,32,128]{3,0,1,2:T(2,128)} %get-tuple-element.48) | copy-start | bytes 1867780
  143.3 1.0 copy-start.1
  143.4 1.4 copy-start.8
Sparse Core Ops, SparseCore 0:
  136.6 33.1 reduce-scatter.1
where the time goes:
time: 180 us; the launch traced here: 178 us
  local copies, waits for them, and re-layouts  50.3 us (28%)
  other arithmetic  48 us (27%)
  waiting for transfers between devices  24.5 us (14%)
  starting transfers between devices  23.9 us (13%)
  blocking collectives  17 us (9%)
  between operations  14.5 us (8%)
    reduce_scatter x1, waiting for transfers between devices, on_device(): lax.psum_scatter(summed, 'scen', scatter_dimension=2, tiled=True)  22.6 us
    all_gather x1, blocking collectives, on_device(): full_kappa = lax.all_gather(diffusivity, 'scen', axis=2, tiled=True)  17 us
    slice x9, local copies, waits for them, and re-layouts, with_halo(): lax.slice_in_dim(block, block.shape[dim] - width, None, axis=dim)  12.6 us
    ppermute x10, starting transfers between devices, from_partner(): lax.ppermute(value, axis, [(i, i ^ 1 << stride) for i in range(lax.axis_s...  11.3 us
    mul x2, other arithmetic, operate_on(): east_flux = east_coeff * (edged_field[..., 1:] - edged_field[..., :-1])  10.4 us
    ppermute x5, starting transfers between devices, with_halo(): lax.ppermute(lax.slice_in_dim(block, 0, width, axis=dim), axis, backward)  9.74 us
    reduce_sum x1, other arithmetic, on_device(): jnp.sum(east_mask[..., 1:] * (before_edge[..., 2:] - before_edge[..., 1:-...  8.7 us
    unnamed x53, local copies, waits for them, and re-layouts  8.08 us
  transfers between devices with their start and end apart: 21, of which 3 were waited for; matrix products, arithmetic and copies ran while one was open for 44% of the time, Pallas kernels for 0%

commit v1 on v0

--- a/solution.py
+++ b/solution.py
@@ -64,7 +64,23 @@
 
 
 def on_device(tracers, diffusivity, level_count, shelf_mask, cotangent):
-    full_kappa = lax.all_gather(diffusivity, "scen", axis=2, tiled=True)
+
+    def kinds_start(base_x, axis_name="scen"):
+        aux, base_arr, z_new = (
+            lax.axis_size(axis_name),
+            lax.axis_index(axis_name),
+            base_x.shape[2],
+        )
+        opened, side_arr = (base_x, 1)
+        while side_arr < aux:
+            row_list = []
+            for hop_no in range(aux):
+                row_list.append((hop_no, (hop_no - side_arr) % aux))
+            opened = jnp.concatenate([opened, lax.ppermute(opened, axis_name, row_list)], 2)
+            side_arr = 2 * side_arr
+        return jnp.roll(opened, base_arr * z_new, axis=2)
+
+    full_kappa = kinds_start(diffusivity)
     levels = lax.broadcasted_iota(jnp.int32, (full_kappa.shape[1],) + level_count.shape, 0)
     wetness = (levels < level_count[None]).astype(jnp.float32)
     sources = sources_of(wetness, shelf_mask)

time: 180 us -> 172 us (0.956)
  blocking collectives: 17 us -> 0 us
  starting transfers between devices: 23.9 us -> 28.9 us
  waiting for transfers between devices: 24.5 us -> 27.7 us
  other arithmetic: 48 us -> 50.3 us
    all_gather x1 -> x0, blocking collectives: 17 us -> none  [on_device(): full_kappa = lax.all_gather(diffusivity, 'scen', axis=2, tiled=True)]
    ppermute x0 -> x3, waiting for transfers between devices: none -> 6.96 us  [kinds_start(): lax.ppermute(opened, axis_name, row_list)]
    concatenate x0 -> x1, local copies, waits for them, and re-layouts: none -> 6.28 us  [kinds_start(): return jnp.roll(opened, base_arr * z_new, axis=2)]
    ppermute x0 -> x3, starting transfers between devices: none -> 5.26 us  [kinds_start(): lax.ppermute(opened, axis_name, row_list)]
    reduce_scatter x1, waiting for transfers between devices: 22.6 us -> 19.6 us  [on_device(): lax.psum_scatter(summed, 'scen', scatter_dimension=2, tiled=True)]
    unnamed x53 -> x58, local copies, waits for them, and re-layouts: 8.08 us -> 5.12 us
    slice x9, local copies, waits for them, and re-layouts: 12.6 us -> 10.5 us  [with_halo(): lax.slice_in_dim(block, block.shape[dim] - width, None, axis=dim)]
    ppermute x10, waiting for transfers between devices: 1.89 us -> 0.03 us  [from_partner(): lax.ppermute(value, axis, [(i, i ^ 1 << stride) for i in range(lax.axis_s...]
  transfers between devices with their start and end apart: 21 -> 24, of which waited for: 3 -> 4; matrix products, arithmetic and copies ran while one was open for 44% -> 44% of each run, Pallas kernels for 0% -> 0%
where the time goes in v1:
time: 172 us; the launch traced here: 171 us
  other arithmetic  50.3 us (29%)
  local copies, waits for them, and re-layouts  49.7 us (29%)
  starting transfers between devices  28.9 us (17%)
  waiting for transfers between devices  27.7 us (16%)
  between operations  14.6 us (8%)
    reduce_scatter x1, waiting for transfers between devices, on_device(): lax.psum_scatter(summed, 'scen', scatter_dimension=2, tiled=True)  19.6 us
    ppermute x10, starting transfers between devices, from_partner(): lax.ppermute(value, axis, [(i, i ^ 1 << stride) for i in range(lax.axis_s...  10.9 us
    slice x9, local copies, waits for them, and re-layouts, with_halo(): lax.slice_in_dim(block, block.shape[dim] - width, None, axis=dim)  10.5 us
    mul x2, other arithmetic, operate_on(): east_flux = east_coeff * (edged_field[..., 1:] - edged_field[..., :-1])  9.29 us
    ppermute x5, starting transfers between devices, with_halo(): lax.ppermute(lax.slice_in_dim(block, 0, width, axis=dim), axis, backward)  8.75 us
    reduce_sum x1, other arithmetic, on_device(): jnp.sum(east_mask[..., 1:] * (before_edge[..., 2:] - before_edge[..., 1:-...  8.62 us
    ppermute x5, local copies, waits for them, and re-layouts, with_halo(): lax.ppermute(lax.slice_in_dim(block, block.shape[dim] - width, None, axis...  7.24 us
    ppermute x3, waiting for transfers between devices, kinds_start(): lax.ppermute(opened, axis_name, row_list)  6.96 us
  transfers between devices with their start and end apart: 24, of which 4 were waited for; matrix products, arithmetic and copies ran while one was open for 44% of the time, Pallas kernels for 0%

profile of v1, /device:TPU:0, one launch (start us, length us, event | category | flops | bytes accessed | tf_op | source)
XLA Modules:
  0.0 171.1 jit_solution(16213194224031375157)
XLA Ops:
  7.2 4.5 %collective-permute-start = (f32[2,20,4,128]{3,2,1,0:T(4,128)}, f32[2,20,4,128]{3,2,1,0:T(4,128)S(1)}, u32[]{:S(2)}, u32[]{:S(2)}) collective-permute-start(f32[2,20,4,128]{3,2,1,0:T(4,128)} %param.6), channel_id=1, source_target_pairs={{0,7},{1,0},{2,1},{3,2},{4,3},{5,4},{6,5},{7,6},{8,15},{9,8},{10,9... | collective-permute-start | bytes 245768 | tf_op jit(solution)/shard_map/ppermute | solution.py:79
  13.5 1.5 collective-permute-start.17
  17.2 2.5 %collective-permute-start.5 = (f32[2,20,32,1]{2,0,3,1:T(2,128)S(1)}, f32[2,20,32,1]{2,0,3,1:T(2,128)S(1)}, u32[]{:S(2)}, u32[]{:S(2)}) collective-permute-start(f32[2,20,32,1]{2,0,3,1:T(2,128)S(1)} %copy.110), channel_id=1, source_target_pairs={{8,0},{16,8},{24,16},{0,24},{9,1},{17,9},{25,17},{1,25},{10,2},{18... | collective-permute-start | bytes 15368 | tf_op jit(solution)/shard_map/ppermute | solution.py:20
  20.3 1.7 %fusion.38 = (f32[2,19,32,128]{3,0,1,2:T(2,128)}, f32[2,19,32,128]{3,0,1,2:T(2,128)}) fusion(f32[2,20,32,128]{3,0,1,2:T(2,128)S(1)} %bitcast_multiply_fusion, f32[19,32,128]{2,0,1:T(8,128)S(1)} %copy.115, f32[2,20,32,128]{3,0,1,2:T(2,128)S(1)} %bitcast.79), kind=kLoop, calls=%fused_computation.78 | loop fusion | flops 622592 | bytes 4046848 | tf_op jit(solution)/shard_map/mul | solution.py:58
  23.7 4.7 %collective-permute-done.1 = f32[2,20,8,128]{3,2,1,0:T(8,128)S(1)} collective-permute-done((f32[2,20,8,128]{3,2,1,0:T(8,128)S(1)}, f32[2,20,8,128]{3,2,1,0:T(8,128)S(1)}, u32[]{:S(2)}, u32[]{:S(2)}) %collective-permute-start.1) | collective-permute-done | bytes 163872 | tf_op jit(solution)/shard_map/ppermute | solution.py:79
  30.6 2.9 %collective-permute-start.15 = (f32[2,20,32,1]{2,0,3,1:T(2,128)S(1)}, f32[2,20,32,1]{2,0,3,1:T(2,128)S(1)}, u32[]{:S(2)}, u32[]{:S(2)}) collective-permute-start(f32[2,20,32,1]{2,0,3,1:T(2,128)S(1)} %copy.122), channel_id=1, source_target_pairs={{8,0},{16,8},{24,16},{0,24},{9,1},{17,9},{25,17},{1,25},{10,2},{18... | collective-permute-start | bytes 15368 | tf_op jit(solution)/shard_map/ppermute | solution.py:20
  34.1 1.5 collective-permute-start.10
  35.6 2.0 %copy.116 = f32[1,20,32,128]{3,0,1,2:T(1,128)} copy(f32[1,20,32,128]{3,2,1,0:T(8,128)} %multiply_bitcast_fusion) | data formatting | bytes 655360 | tf_op jit(solution)/shard_map/stack | solution.py:43
  38.2 1.2 copy.113
  39.3 1.2 copy.123
  40.5 1.2 copy.125
  41.9 2.3 %collective-permute-done.2 = f32[2,20,16,128]{3,2,1,0:T(8,128)} collective-permute-done((f32[2,20,16,128]{3,2,1,0:T(8,128)}, f32[2,20,16,128]{3,2,1,0:T(8,128)}, u32[]{:S(2)}, u32[]{:S(2)}) %collective-permute-start.2) | collective-permute-done | bytes 327712 | tf_op jit(solution)/shard_map/ppermute | solution.py:79
  44.2 6.3 %concatenate.108 = f32[2,20,64,128]{3,2,1,0:T(8,128)} concatenate(f32[2,20,4,128]{3,2,1,0:T(4,128)S(1)} %copy-done.22, f32[2,20,4,128]{3,2,1,0:T(4,128)S(1)} %collective-permute-done, f32[2,20,8,128]{3,2,1,0:T(8,128)S(1)} %collective-permute-done.1, f32[2,20,16,128]{3,2,1,0:T(8,128)} %collective-permute-done.2, f32[2,20,4,128]{3,2,1,0:T(4,128)S(1)} %copy-done.22, ...), dimensions={2} | concatenate | bytes 2621440 | tf_op jit(solution)/shard_map/jit(_roll_dynamic)/concatenate | solution.py:81
  50.5 1.1 dynamic-slice_bitcast_fusion
  52.5 1.4 collective-permute-start.7
  54.1 1.3 slice_maximum_fusion
  55.4 1.4 copy.105
  56.7 1.4 copy.106
  60.2 1.6 subtract_multiply_fusion.1
  63.9 1.2 copy.107
  65.0 1.2 copy.108
  66.2 1.9 %pad_maximum_fusion.4 = f32[2,20,32,130]{3,2,1,0:T(8,128)S(1)} fusion(f32[2,20,32,1]{3,2,1,0:T(8,128)} %copy.108, f32[1,20,32,128]{3,2,1,0:T(8,128)S(1)} %get-tuple-element.23, f32[1,20,32,128]{3,2,1,0:T(8,128)S(1)} %fusion.42, f32[2,20,32,1]{3,2,1,0:T(8,128)} %copy.107), kind=kLoop, calls=%fused_computation.20 | loop fusion | flops 499200 | bytes 1331200 | tf_op jit(solution)/shard_map/concatenate | solution.py:21
  68.9 1.2 collective-permute-start.8
  70.1 4.5 %fusion.3 = (f32[2,20,32,129]{3,0,1,2:T(2,128)}, f32[2,20,32,129]{3,0,1,2:T(2,128)}) fusion(f32[2,20,32,1]{3,0,1,2:T(2,128)S(1)} %copy-done.3, f32[2,20,32,128]{3,0,1,2:T(2,128)S(1)} %bitcast_multiply_fusion, f32[2,20,32,1]{3,0,1,2:T(2,128)S(1)} %copy-done.13, f32[20,32,129]{2,0,1:T(8,128)S(1)} %copy.109, f32[2,20,32,128]{3,0,1,2:T(2,128)S(1)} %bitcast.81, ...), kind=kLoop, calls=%fused_computation.15 | loop fusion | flops 1320960 | bytes 2982400 | tf_op jit(solution)/shard_map/mul | solution.py:49
  76.9 6.2 %fusion.33 = (f32[2,20,32,128]{3,0,1,2:T(2,128)S(1)}, f32[2,20,32,128]{3,0,1,2:T(2,128)S(1)}) fusion(f32[2,19,32,128]{3,0,1,2:T(2,128)} %get-tuple-element.48, f32[2,20,31,128]{3,0,1,2:T(2,128)} %get-tuple-element.50, f32[2,20,1,128]{3,0,1,2:T(2,128)S(1)} %get-tuple-element.58, f32[2,20,32,129]{3,0,1,2:T(2,128)} %get-tuple-element.28, ...), kind=kLoop, calls=%fused_computation.65 | loop fusion | flops 2949120 | bytes 8454144 | tf_op jit(solution)/shard_map/mul | solution.py:111
  83.2 1.7 %fusion.44 = (f32[2,20,32,1]{3,0,1,2:T(2,128)}, f32[2,20,32,1]{3,0,1,2:T(2,128)}) fusion(f32[2,20,32,128]{3,0,1,2:T(2,128)S(1)} %get-tuple-element.46), kind=kLoop, calls=%fused_computation.118 | loop fusion | bytes 20480 | tf_op jit(solution)/shard_map/slice | solution.py:18
  84.9 1.8 %fusion.46 = (f32[2,20,32,1]{3,0,1,2:T(2,128)}, f32[2,20,32,1]{3,0,1,2:T(2,128)}) fusion(f32[2,20,32,128]{3,0,1,2:T(2,128)S(1)} %get-tuple-element.47), kind=kLoop, calls=%fused_computation.120 | loop fusion | bytes 20480 | tf_op jit(solution)/shard_map/slice | solution.py:18
  87.2 1.5 collective-permute-start.21
  88.7 6.7 %multiply_reduce_fusion = (f32[20,31,128]{2,0,1:T(8,128)}, f32[20,31,128]{2,0,1:T(8,128)}, f32[2,20,31,128]{3,0,1,2:T(2,128)}, f32[2,20,31,128]{3,0,1,2:T(2,128)}) fusion(f32[2,20,32,128]{3,0,1,2:T(2,128)S(1)} %get-tuple-element.46, f32[20,31,128]{2,0,1:T(8,128)S(1)} %copy-done.20, f32[2,20,32,128]{3,0,1,2:T(2,128)S(1)} %bitcast.83, ...), kind=kLoop, calls=%fused_computation.71 | loop fusion | flops 1904640 | bytes 7618560 | tf_op jit(solution)/shard_map/reduce_sum | solution.py:121
  95.4 2.0 %copy.126 = f32[2,20,32,1]{2,0,3,1:T(2,128)} copy(f32[2,20,32,1]{3,0,1,2:T(2,128)} %get-tuple-element.35) | data formatting | bytes 10240 | tf_op jit(solution)/shard_map/slice | solution.py:20
  98.2 2.0 %copy.117 = f32[2,20,32,1]{2,0,3,1:T(2,128)} copy(f32[2,20,32,1]{3,0,1,2:T(2,128)} %get-tuple-element.39) | data formatting | bytes 10240 | tf_op jit(solution)/shard_map/slice | solution.py:20
  100.2 1.5 collective-permute-start.11
  101.7 2.7 %fusion.37 = (f32[2,19,32,128]{3,0,1,2:T(2,128)}, f32[2,19,32,128]{3,0,1,2:T(2,128)}) fusion(f32[2,20,32,128]{3,0,1,2:T(2,128)S(1)} %get-tuple-element.46, f32[19,32,128]{2,0,1:T(8,128)} %copy-done.6, f32[2,20,32,128]{3,0,1,2:T(2,128)S(1)} %get-tuple-element.47), kind=kLoop, calls=%fused_computation.76 | loop fusion | flops 622592 | bytes 4046848 | tf_op jit(solution)/shard_map/mul | solution.py:58
  104.4 1.4 copy.128
  106.6 2.0 %copy.119 = f32[2,20,32,1]{2,0,3,1:T(2,128)} copy(f32[2,20,32,1]{3,0,1,2:T(2,128)} %get-tuple-element.38) | data formatting | bytes 10240 | tf_op jit(solution)/shard_map/slice | solution.py:18
  108.6 2.1 %collective-permute-start.12 = (f32[2,20,32,1]{2,0,3,1:T(2,128)}, f32[2,20,32,1]{2,0,3,1:T(2,128)}, u32[]{:S(2)}, u32[]{:S(2)}) collective-permute-start(f32[2,20,32,1]{2,0,3,1:T(2,128)} %copy.119), channel_id=1, source_target_pairs={{0,8},{8,16},{16,24},{24,0},{1,9},{9,17},{17,25},{25,1},{2,10},{10... | collective-permute-start | bytes 15368 | tf_op jit(solution)/shard_map/ppermute | solution.py:17
  110.7 1.9 %copy.127 = f32[2,20,32,1]{3,0,1,2:T(2,128)} copy(f32[2,20,32,1]{2,0,3,1:T(2,128)} %collective-permute-done.19) | data formatting | bytes 10240 | tf_op jit(solution)/shard_map/ppermute | solution.py:20
  112.6 1.9 %copy.118 = f32[2,20,32,1]{3,0,1,2:T(2,128)} copy(f32[2,20,32,1]{2,0,3,1:T(2,128)} %collective-permute-done.11) | data formatting | bytes 10240 | tf_op jit(solution)/shard_map/ppermute | solution.py:20
  115.3 1.2 collective-permute-start.22
  116.5 8.6 %fusion.36 = (f32[20,32,128]{2,0,1:T(8,128)}, f32[20,32,128]{2,0,1:T(8,128)}) fusion(f32[2,20,32,128]{3,0,1,2:T(2,128)S(1)} %get-tuple-element.46, f32[2,20,32,1]{3,0,1,2:T(2,128)} %copy.127, f32[2,20,32,128]{3,0,1,2:T(2,128)S(1)} %bitcast.84, f32[2,20,32,1]{3,0,1,2:T(2,128)} %copy-done.2, f32[20,32,128]{2,0,1:T(8,128)} %copy.130, ...), kind=kLoop, calls=%fused_computation.68 | loop fusion | flops 2129920 | bytes 3624960 | tf_op jit(solution)/shard_map/reduce_sum | solution.py:115
  125.1 1.9 %copy.129 = f32[2,20,32,1]{3,0,1,2:T(2,128)} copy(f32[2,20,32,1]{2,0,3,1:T(2,128)} %collective-permute-done.20) | data formatting | bytes 10240 | tf_op jit(solution)/shard_map/ppermute | solution.py:17
  127.0 1.9 %copy.120 = f32[2,20,32,1]{3,0,1,2:T(2,128)} copy(f32[2,20,32,1]{2,0,3,1:T(2,128)} %collective-permute-done.12) | data formatting | bytes 10240 | tf_op jit(solution)/shard_map/ppermute | solution.py:17
  129.2 1.1 maximum_bitcast_fusion.1
  133.0 4.8 %fusion.1 = (f32[2,20,32,129]{3,0,1,2:T(2,128)S(1)}, f32[2,20,32,129]{3,0,1,2:T(2,128)S(1)}) fusion(f32[2,20,32,1]{3,0,1,2:T(2,128)S(1)} %copy-done.4, f32[2,20,32,128]{3,0,1,2:T(2,128)S(1)} %get-tuple-element.46, f32[2,20,32,1]{3,0,1,2:T(2,128)} %copy.129, f32[20,32,129]{2,0,1:T(8,128)S(1)} %copy.109, f32[2,20,32,128]{3,0,1,2:T(2,128)S(1)} %get-tuple-element.47, ...), kind=kLoop, calls=%fused_computation.13 | loop fusion | flops 1320960 | bytes 2982400 | tf_op jit(solution)/shard_map/mul | solution.py:49
  137.9 1.4 fusion.34
  140.6 1.6 fusion.10
  143.1 19.6 %reduce-scatter.2.cloned.1.call-done = f32[2,20,4,128]{3,1,0,2:T(8,128)} async-done(((f32[2,20,32,128]{3,1,0,2:T(8,128)}), f32[2,20,4,128]{3,1,0,2:T(8,128)}) %reduce-scatter.2.cloned.1.call-update) | async-done | bytes 81936 | tf_op jit(solution)/shard_map/reduce_scatter | solution.py:138
  162.7 1.6 copy.135
  (136 shorter events, 26.2 us)
Async XLA Ops:
  7.2 5.6 %copy-start.10 = (f32[1,2,20,32,128]{4,3,2,1,0:T(8,128)S(1)}, f32[1,2,20,32,128]{4,3,2,1,0:T(8,128)}, u32[]{:S(2)}) copy-start(f32[1,2,20,32,128]{4,3,2,1,0:T(8,128)} %param.9) | copy-start | bytes 1966084
  7.2 155.6 %reduce-scatter.2.cloned.1.call-start = ((), (), s32[]{:S(2)}) async-start(), calls=%async_computation.1 | async-start | bytes 884736 | tf_op jit(solution)/shard_map/reduce_scatter | solution.py:138
  7.2 15.6 %collective-permute-start = (f32[2,20,4,128]{3,2,1,0:T(4,128)}, f32[2,20,4,128]{3,2,1,0:T(4,128)S(1)}, u32[]{:S(2)}, u32[]{:S(2)}) collective-permute-start(f32[2,20,4,128]{3,2,1,0:T(4,128)} %param.6), channel_id=1, source_target_pairs={{0,7},{1,0},{2,1},{3,2},{4,3},{5,4},{6,5},{7,6},{8,15},{9,8},{10,9... | collective-permute-start | bytes 245768 | tf_op jit(solution)/shard_map/ppermute | solution.py:79
  12.5 2.5 %copy-start.11 = (f32[1,2,20,32,128]{4,3,2,1,0:T(8,128)S(1)}, f32[1,2,20,32,128]{4,3,2,1,0:T(8,128)}, u32[]{:S(2)}) copy-start(f32[1,2,20,32,128]{4,3,2,1,0:T(8,128)} %param.5) | copy-start | bytes 1966084
  13.5 20.0 %collective-permute-start.17 = (f32[2,20,128]{2,0,1:T(2,128)S(1)}, f32[2,20,128]{2,0,1:T(2,128)S(1)}, u32[]{:S(2)}, u32[]{:S(2)}) collective-permute-start(f32[2,20,128]{2,0,1:T(2,128)S(1)} %slice_bitcast_fusion.3), channel_id=1, source_target_pairs={{0,8},{8,0},{16,24},{24,16},{1,9},{9,1},{17,25},{25,17},{2,10},{10... | collective-permute-start | bytes 61448 | tf_op jit(solution)/shard_map/ppermute | solution.py:26
  15.5 18.6 %collective-permute-start.9 = (f32[2,20,128]{2,0,1:T(2,128)S(1)}, f32[2,20,128]{2,0,1:T(2,128)S(1)}, u32[]{:S(2)}, u32[]{:S(2)}) collective-permute-start(f32[2,20,128]{2,0,1:T(2,128)S(1)} %slice_bitcast_fusion.5), channel_id=1, source_target_pairs={{0,8},{8,0},{16,24},{24,16},{1,9},{9,1},{17,25},{25,17},{2,10},{10... | collective-permute-start | bytes 61448 | tf_op jit(solution)/shard_map/ppermute | solution.py:26
  17.2 13.4 %collective-permute-start.5 = (f32[2,20,32,1]{2,0,3,1:T(2,128)S(1)}, f32[2,20,32,1]{2,0,3,1:T(2,128)S(1)}, u32[]{:S(2)}, u32[]{:S(2)}) collective-permute-start(f32[2,20,32,1]{2,0,3,1:T(2,128)S(1)} %copy.110), channel_id=1, source_target_pairs={{8,0},{16,8},{24,16},{0,24},{9,1},{17,9},{25,17},{1,25},{10,2},{18... | collective-permute-start | bytes 15368 | tf_op jit(solution)/shard_map/ppermute | solution.py:20
  20.0 13.5 %collective-permute-start.6 = (f32[2,20,32,1]{2,0,3,1:T(2,128)S(1)}, f32[2,20,32,1]{2,0,3,1:T(2,128)S(1)}, u32[]{:S(2)}, u32[]{:S(2)}) collective-permute-start(f32[2,20,32,1]{2,0,3,1:T(2,128)S(1)} %copy.112), channel_id=1, source_target_pairs={{0,8},{8,16},{16,24},{24,0},{1,9},{9,17},{17,25},{25,1},{2,10},{10... | collective-permute-start | bytes 15368 | tf_op jit(solution)/shard_map/ppermute | solution.py:17
  20.3 1.7 %copy-start.6 = (f32[19,32,128]{2,0,1:T(8,128)}, f32[19,32,128]{2,0,1:T(8,128)S(1)}, u32[]{:S(2)}) copy-start(f32[19,32,128]{2,0,1:T(8,128)S(1)} %copy.115) | copy-start | bytes 933892
  22.0 1.6 copy-start.25
  22.0 7.1 %copy-start.24 = (s32[32,128]{1,0:T(8,128)S(1)}, s32[32,128]{1,0:T(8,128)}, u32[]{:S(2)}) copy-start(s32[32,128]{1,0:T(8,128)} %param.7) | copy-start | bytes 49156
  23.0 5.4 %collective-permute-start.1 = (f32[2,20,8,128]{3,2,1,0:T(8,128)S(1)}, f32[2,20,8,128]{3,2,1,0:T(8,128)S(1)}, u32[]{:S(2)}, u32[]{:S(2)}) collective-permute-start(f32[2,20,8,128]{3,2,1,0:T(8,128)S(1)} %pad_maximum_fusion.7), channel_id=1, source_target_pairs={{0,6},{1,7},{2,0},{3,1},{4,2},{5,3},{6,4},{7,5},{8,14},{9,15},{10,... | collective-permute-start | bytes 491528 | tf_op jit(solution)/shard_map/ppermute | solution.py:79
  29.1 15.1 %collective-permute-start.2 = (f32[2,20,16,128]{3,2,1,0:T(8,128)}, f32[2,20,16,128]{3,2,1,0:T(8,128)}, u32[]{:S(2)}, u32[]{:S(2)}) collective-permute-start(f32[2,20,16,128]{3,2,1,0:T(8,128)} %pad_maximum_fusion.6), channel_id=1, source_target_pairs={{0,4},{1,5},{2,6},{3,7},{4,0},{5,1},{6,2},{7,3},{8,12},{9,13},{10,... | collective-permute-start | bytes 983048 | tf_op jit(solution)/shard_map/ppermute | solution.py:79
  30.6 8.8 %collective-permute-start.15 = (f32[2,20,32,1]{2,0,3,1:T(2,128)S(1)}, f32[2,20,32,1]{2,0,3,1:T(2,128)S(1)}, u32[]{:S(2)}, u32[]{:S(2)}) collective-permute-start(f32[2,20,32,1]{2,0,3,1:T(2,128)S(1)} %copy.122), channel_id=1, source_target_pairs={{8,0},{16,8},{24,16},{0,24},{9,1},{17,9},{25,17},{1,25},{10,2},{18... | collective-permute-start | bytes 15368 | tf_op jit(solution)/shard_map/ppermute | solution.py:20
  33.5 7.0 %collective-permute-start.16 = (f32[2,20,32,1]{2,0,3,1:T(2,128)S(1)}, f32[2,20,32,1]{2,0,3,1:T(2,128)S(1)}, u32[]{:S(2)}, u32[]{:S(2)}) collective-permute-start(f32[2,20,32,1]{2,0,3,1:T(2,128)S(1)} %copy.124), channel_id=1, source_target_pairs={{0,8},{8,16},{16,24},{24,0},{1,9},{9,17},{17,25},{25,1},{2,10},{10... | collective-permute-start | bytes 15368 | tf_op jit(solution)/shard_map/ppermute | solution.py:17
  33.5 8.2 %collective-permute-start.18 = (f32[2,20,128]{2,0,1:T(2,128)S(1)}, f32[2,20,128]{2,0,1:T(2,128)S(1)}, u32[]{:S(2)}, u32[]{:S(2)}) collective-permute-start(f32[2,20,128]{2,0,1:T(2,128)S(1)} %collective-permute-done.17), channel_id=1, source_target_pairs={{0,16},{8,24},{16,0},{24,8},{1,17},{9,25},{17,1},{25,9},{2,18},{10... | collective-permute-start | bytes 61448 | tf_op jit(solution)/shard_map/ppermute | solution.py:26
  34.1 7.6 %collective-permute-start.10 = (f32[2,20,128]{2,0,1:T(2,128)S(1)}, f32[2,20,128]{2,0,1:T(2,128)S(1)}, u32[]{:S(2)}, u32[]{:S(2)}) collective-permute-start(f32[2,20,128]{2,0,1:T(2,128)S(1)} %collective-permute-done.9), channel_id=1, source_target_pairs={{0,16},{8,24},{16,0},{24,8},{1,17},{9,25},{17,1},{25,9},{2,18},{10... | collective-permute-start | bytes 61448 | tf_op jit(solution)/shard_map/ppermute | solution.py:26
  38.2 32.0 %copy-start.2 = (f32[2,20,32,1]{3,0,1,2:T(2,128)}, f32[2,20,32,1]{3,0,1,2:T(2,128)S(1)}, u32[]{:S(2)}) copy-start(f32[2,20,32,1]{3,0,1,2:T(2,128)S(1)} %copy.111) | copy-start | bytes 15364
  51.6 2.3 %copy-start.21 = (f32[20,32,128]{2,1,0:T(8,128)}, f32[20,32,128]{2,1,0:T(8,128)S(1)}, u32[]{:S(2)}) copy-start(f32[20,32,128]{2,1,0:T(8,128)S(1)} %get-tuple-element.22) | copy-start | bytes 983044
  52.5 16.4 %collective-permute-start.7 = (f32[2,20,128]{2,0,1:T(2,128)S(1)}, f32[2,20,128]{2,0,1:T(2,128)S(1)}, u32[]{:S(2)}, u32[]{:S(2)}) collective-permute-start(f32[2,20,128]{2,0,1:T(2,128)S(1)} %pad_maximum_fusion.8), channel_id=1, source_target_pairs={{0,8},{8,0},{16,24},{24,16},{1,9},{9,1},{17,25},{25,17},{2,10},{10... | collective-permute-start | bytes 61448 | tf_op jit(solution)/shard_map/ppermute | solution.py:26
  54.1 6.1 %copy-start.7 = (f32[20,31,128]{2,0,1:T(8,128)}, f32[20,31,128]{2,0,1:T(8,128)S(1)}, u32[]{:S(2)}) copy-start(f32[20,31,128]{2,0,1:T(8,128)S(1)} %copy.114) | copy-start | bytes 952324
  58.1 3.7 %copy-start.23 = (f32[20,31,128]{2,1,0:T(8,128)S(1)}, f32[20,31,128]{2,1,0:T(8,128)}, u32[]{:S(2)}) copy-start(f32[20,31,128]{2,1,0:T(8,128)} %get-tuple-element.19) | copy-start | bytes 952324
  58.1 6.9 %collective-permute-start.4 = (f32[2,20,32,1]{2,0,3,1:T(2,128)S(1)}, f32[2,20,32,1]{2,0,3,1:T(2,128)S(1)}, u32[]{:S(2)}, u32[]{:S(2)}) collective-permute-start(f32[2,20,32,1]{2,0,3,1:T(2,128)S(1)} %copy.106), channel_id=1, source_target_pairs={{8,0},{16,8},{24,16},{0,24},{9,1},{17,9},{25,17},{1,25},{10,2},{18... | collective-permute-start | bytes 15368 | tf_op jit(solution)/shard_map/ppermute | solution.py:20
  59.2 4.7 %collective-permute-start.3 = (f32[2,20,32,1]{2,0,3,1:T(2,128)S(1)}, f32[2,20,32,1]{2,0,3,1:T(2,128)S(1)}, u32[]{:S(2)}, u32[]{:S(2)}) collective-permute-start(f32[2,20,32,1]{2,0,3,1:T(2,128)S(1)} %copy.105), channel_id=1, source_target_pairs={{0,8},{8,16},{16,24},{24,0},{1,9},{9,17},{17,25},{25,1},{2,10},{10... | collective-permute-start | bytes 15368 | tf_op jit(solution)/shard_map/ppermute | solution.py:17
  68.2 1.9 %copy-start.13 = (f32[2,20,32,1]{3,0,1,2:T(2,128)S(1)}, f32[2,20,32,1]{3,0,1,2:T(2,128)}, u32[]{:S(2)}) copy-start(f32[2,20,32,1]{3,0,1,2:T(2,128)} %copy.125) | copy-start | bytes 15364
  68.5 1.7 copy-start.3
  68.5 1.7 copy-start.12
  68.9 6.8 %collective-permute-start.8 = (f32[2,20,128]{2,0,1:T(2,128)S(1)}, f32[2,20,128]{2,0,1:T(2,128)S(1)}, u32[]{:S(2)}, u32[]{:S(2)}) collective-permute-start(f32[2,20,128]{2,0,1:T(2,128)S(1)} %collective-permute-done.7), channel_id=1, source_target_pairs={{0,16},{8,24},{16,0},{24,8},{1,17},{9,25},{17,1},{25,9},{2,18},{10... | collective-permute-start | bytes 61448 | tf_op jit(solution)/shard_map/ppermute | solution.py:26
  84.9 3.8 %copy-start.8 = (f32[20,31,128]{2,0,1:T(8,128)S(1)}, f32[20,31,128]{2,0,1:T(8,128)}, u32[]{:S(2)}) copy-start(f32[20,31,128]{2,0,1:T(8,128)} %copy-done.7) | copy-start | bytes 952324
  84.9 3.8 %copy-start.20 = (f32[20,31,128]{2,0,1:T(8,128)S(1)}, f32[20,31,128]{2,0,1:T(8,128)}, u32[]{:S(2)}) copy-start(f32[20,31,128]{2,0,1:T(8,128)} %copy.131) | copy-start | bytes 952324
  86.7 27.7 %collective-permute-start.13 = (f32[2,20,128]{2,0,1:T(2,128)S(1)}, f32[2,20,128]{2,0,1:T(2,128)}, u32[]{:S(2)}, u32[]{:S(2)}) collective-permute-start(f32[2,20,128]{2,0,1:T(2,128)S(1)} %slice_bitcast_fusion.4), channel_id=1, source_target_pairs={{0,8},{8,0},{16,24},{24,16},{1,9},{9,1},{17,25},{25,17},{2,10},{10... | collective-permute-start | bytes 61448 | tf_op jit(solution)/shard_map/ppermute | solution.py:26
  87.2 28.1 %collective-permute-start.21 = (f32[2,20,128]{2,0,1:T(2,128)S(1)}, f32[2,20,128]{2,0,1:T(2,128)}, u32[]{:S(2)}, u32[]{:S(2)}) collective-permute-start(f32[2,20,128]{2,0,1:T(2,128)S(1)} %slice_bitcast_fusion.2), channel_id=1, source_target_pairs={{0,8},{8,0},{16,24},{24,16},{1,9},{9,1},{17,25},{25,17},{2,10},{10... | collective-permute-start | bytes 61448 | tf_op jit(solution)/shard_map/ppermute | solution.py:26
  97.4 11.2 %collective-permute-start.19 = (f32[2,20,32,1]{2,0,3,1:T(2,128)}, f32[2,20,32,1]{2,0,3,1:T(2,128)}, u32[]{:S(2)}, u32[]{:S(2)}) collective-permute-start(f32[2,20,32,1]{2,0,3,1:T(2,128)} %copy.126), channel_id=1, source_target_pairs={{8,0},{16,8},{24,16},{0,24},{9,1},{17,9},{25,17},{1,25},{10,2},{18... | collective-permute-start | bytes 15368 | tf_op jit(solution)/shard_map/ppermute | solution.py:20
  100.2 12.3 %collective-permute-start.11 = (f32[2,20,32,1]{2,0,3,1:T(2,128)}, f32[2,20,32,1]{2,0,3,1:T(2,128)}, u32[]{:S(2)}, u32[]{:S(2)}) collective-permute-start(f32[2,20,32,1]{2,0,3,1:T(2,128)} %copy.117), channel_id=1, source_target_pairs={{8,0},{16,8},{24,16},{0,24},{9,1},{17,9},{25,17},{1,25},{10,2},{18... | collective-permute-start | bytes 15368 | tf_op jit(solution)/shard_map/ppermute | solution.py:20
  105.8 19.3 %collective-permute-start.20 = (f32[2,20,32,1]{2,0,3,1:T(2,128)S(1)}, f32[2,20,32,1]{2,0,3,1:T(2,128)}, u32[]{:S(2)}, u32[]{:S(2)}) collective-permute-start(f32[2,20,32,1]{2,0,3,1:T(2,128)S(1)} %copy.128), channel_id=1, source_target_pairs={{0,8},{8,16},{16,24},{24,0},{1,9},{9,17},{17,25},{25,1},{2,10},{10... | collective-permute-start | bytes 15368 | tf_op jit(solution)/shard_map/ppermute | solution.py:17
  108.6 18.4 %collective-permute-start.12 = (f32[2,20,32,1]{2,0,3,1:T(2,128)}, f32[2,20,32,1]{2,0,3,1:T(2,128)}, u32[]{:S(2)}, u32[]{:S(2)}) collective-permute-start(f32[2,20,32,1]{2,0,3,1:T(2,128)} %copy.119), channel_id=1, source_target_pairs={{0,8},{8,16},{16,24},{24,0},{1,9},{9,17},{17,25},{25,1},{2,10},{10... | collective-permute-start | bytes 15368 | tf_op jit(solution)/shard_map/ppermute | solution.py:17
  114.4 14.4 %collective-permute-start.14 = (f32[2,20,128]{2,0,1:T(2,128)}, f32[2,20,128]{2,0,1:T(2,128)S(1)}, u32[]{:S(2)}, u32[]{:S(2)}) collective-permute-start(f32[2,20,128]{2,0,1:T(2,128)} %collective-permute-done.13), channel_id=1, source_target_pairs={{0,16},{8,24},{16,0},{24,8},{1,17},{9,25},{17,1},{25,9},{2,18},{10... | collective-permute-start | bytes 61448 | tf_op jit(solution)/shard_map/ppermute | solution.py:26
  115.3 13.7 %collective-permute-start.22 = (f32[2,20,128]{2,0,1:T(2,128)}, f32[2,20,128]{2,0,1:T(2,128)S(1)}, u32[]{:S(2)}, u32[]{:S(2)}) collective-permute-start(f32[2,20,128]{2,0,1:T(2,128)} %collective-permute-done.21), channel_id=1, source_target_pairs={{0,16},{8,24},{16,0},{24,8},{1,17},{9,25},{17,1},{25,9},{2,18},{10... | collective-permute-start | bytes 61448 | tf_op jit(solution)/shard_map/ppermute | solution.py:26
  129.1 2.2 %copy-start.18 = (f32[20,32,128]{2,0,1:T(8,128)S(1)}, f32[20,32,128]{2,0,1:T(8,128)}, u32[]{:S(2)}) copy-start(f32[20,32,128]{2,0,1:T(8,128)} %get-tuple-element.12) | copy-start | bytes 983044
  129.1 2.2 %copy-start.19 = (f32[20,32,128]{2,0,1:T(8,128)S(1)}, f32[20,32,128]{2,0,1:T(8,128)}, u32[]{:S(2)}) copy-start(f32[20,32,128]{2,0,1:T(8,128)} %get-tuple-element.13) | copy-start | bytes 983044
  131.5 1.4 copy-start.4
  131.5 1.6 copy-start.5
  133.0 4.8 %copy-start.15 = (f32[2,20,31,128]{3,0,1,2:T(2,128)S(1)}, f32[2,20,31,128]{3,0,1,2:T(2,128)}, u32[]{:S(2)}) copy-start(f32[2,20,31,128]{3,0,1,2:T(2,128)} %get-tuple-element.33) | copy-start | bytes 1904644
  133.0 4.8 %copy-start.17 = (f32[2,19,32,128]{3,0,1,2:T(2,128)S(1)}, f32[2,19,32,128]{3,0,1,2:T(2,128)}, u32[]{:S(2)}) copy-start(f32[2,19,32,128]{3,0,1,2:T(2,128)} %get-tuple-element.44) | copy-start | bytes 1867780
  137.9 2.4 %copy-start.14 = (f32[2,20,31,128]{3,0,1,2:T(2,128)S(1)}, f32[2,20,31,128]{3,0,1,2:T(2,128)}, u32[]{:S(2)}) copy-start(f32[2,20,31,128]{3,0,1,2:T(2,128)} %get-tuple-element.32) | copy-start | bytes 1904644
  137.9 2.4 %copy-start.16 = (f32[2,19,32,128]{3,0,1,2:T(2,128)S(1)}, f32[2,19,32,128]{3,0,1,2:T(2,128)}, u32[]{:S(2)}) copy-start(f32[2,19,32,128]{3,0,1,2:T(2,128)} %get-tuple-element.45) | copy-start | bytes 1867780
  139.3 1.0 copy-start.1
  139.3 1.2 copy-start.9
  (2 other events, 1.7 us)
Sparse Core Ops, SparseCore 0:
  132.6 30.1 reduce-scatter.1
